TPU v7x, 32 devices: a whole 2x2x4 slice. The times are simulated.
32 devices in a mesh: groups: 2 (over y), pix: 4 (over z), sub: 2 (over x), inner: 2 (over core).
Axes of the slice: x: 2, y: 2, z: 4, core: 2. Of those that a mesh axis runs over, the one named last changes fastest.
Arguments:
- cube: bfloat16 [20480, 256], P(('groups', 'pix', 'sub', 'inner')), parts along dimension 0, may hold values from -70 to 70
Outputs:
- spectra: bfloat16 [256, 16, 1280], P(('pix', 'sub'), 'groups', 'inner'), parts along dimension 1
There are 2 independent parts, one for each index of `groups`. A program takes and returns all parts, laid end to end along the dimension named above; each array names one. Nothing has to cross between parts.
All inputs are finite; a program needn't handle non-finite values.
Results may differ from a plain program's by a relative error of at most 0.0067.
Values may be sent and summed in bfloat16 or wider, within the bound.
No kernel may reach another device: no remote copies, remote signals or barrier semaphores. Data moves between devices by JAX's collectives and lax.ppermute only.
A program may use at most 64 MiB of HBM per device.

v0:
```python
import math
import jax
import jax.numpy as jnp
from jax import lax
from jax.sharding import PartitionSpec as P

MODES = 32
ITERS = 4
VARIANT = "symbutterfly"


def matmul_high(left, right):
    return jnp.dot(left, right, precision=lax.Precision.HIGHEST)


def leading_modes(gram_matrix, width_count, sweeps):
    mode_basis = jnp.eye(gram_matrix.shape[0], width_count, dtype=jnp.float32)
    for iteration in range(sweeps):
        product = matmul_high(gram_matrix, mode_basis)
        cross_gram = matmul_high(product.T, product)
        lower_factor = jnp.linalg.cholesky(cross_gram)
        mode_basis = jax.scipy.linalg.solve_triangular(lower_factor, product.T, lower=True).T
    return mode_basis


def delay_table(channels):
    middle = channels // 2
    row_index = lax.broadcasted_iota(jnp.int32, (channels, channels), 0)
    col_index = lax.broadcasted_iota(jnp.int32, (channels, channels), 1)
    harmonic = jnp.where(row_index <= middle, row_index, row_index - middle)
    angles = (harmonic * col_index % channels).astype(jnp.float32) * (2.0 * math.pi / channels)
    values = jnp.where(row_index <= middle, jnp.cos(angles), jnp.sin(angles)) / math.sqrt(channels)
    return values.astype(jnp.bfloat16)


def steps_of(sizes):
    out = []
    for name, n in sizes:
        d = 1
        while d < n:
            out.append((name, n, d))
            d *= 2
    return out


def butterfly_sum(x, sizes):
    for name, n, d in steps_of(sizes):
        x = x + lax.ppermute(x, name, [(i, i ^ d) for i in range(n)])
    return x


def halving_sum(x, sizes):
    steps = steps_of(sizes)
    for name, n, d in steps:
        bit = lax.axis_index(name) // d % 2
        half = x.shape[0] // 2
        lo, hi = (x[:half], x[half:])
        send = jnp.where(bit == 0, hi, lo)
        keep = jnp.where(bit == 0, lo, hi)
        x = keep + lax.ppermute(send, name, [(i, i ^ d) for i in range(n)])
    for name, n, d in reversed(steps):
        bit = lax.axis_index(name) // d % 2
        other = lax.ppermute(x, name, [(i, i ^ d) for i in range(n)])
        x = jnp.where(bit == 0, jnp.concatenate([x, other]), jnp.concatenate([other, x]))
    return x


def make_local(sizes):

    def reduce(g):
        if VARIANT == "psum":
            return lax.psum(g, ("pix", "sub", "inner"))
        if VARIANT == "butterfly":
            return butterfly_sum(g, sizes)
        if VARIANT == "halving":
            return halving_sum(g, sizes)
        if VARIANT == "symbutterfly":
            h = g.shape[0] // 2
            packed = jnp.concatenate([g[:h, :h], g[:h, h:], g[h:, h:]], axis=0)
            packed = butterfly_sum(packed, sizes)
            a, b, d = (packed[:h], packed[h : 2 * h], packed[2 * h :])
            return jnp.concatenate([jnp.concatenate([a, b], 1), jnp.concatenate([b.T, d], 1)], 0)
        raise ValueError(VARIANT)

    def local(cube):
        pixels, channels = cube.shape
        pixel_count = pixels * lax.axis_size(("pix", "sub", "inner"))
        partial_gram = lax.dot_general(
            cube, cube, (((0,), (0,)), ((), ())), preferred_element_type=jnp.float32
        )
        gram_matrix = reduce(partial_gram)
        gram_matrix = gram_matrix / pixel_count
        mode_basis = leading_modes(gram_matrix, MODES, ITERS)
        modes_b = mode_basis.astype(jnp.bfloat16)
        amplitudes = jnp.dot(cube, modes_b, preferred_element_type=jnp.float32).astype(jnp.bfloat16)
        cleaned = (
            cube - jnp.dot(amplitudes, modes_b.T, preferred_element_type=jnp.float32)
        ).astype(jnp.bfloat16)
        table_b = delay_table(channels)
        coefficients = lax.dot_general(
            table_b, cleaned, (((1,), (1,)), ((), ())), preferred_element_type=jnp.float32
        ).astype(jnp.bfloat16)
        spectra = lax.all_to_all(
            coefficients[:, None, :], ("pix", "sub"), split_axis=0, concat_axis=1, tiled=True
        )
        return spectra

    return local


def solution(mesh):
    sizes = [(a, mesh.shape[a]) for a in ("inner", "sub", "pix")]
    return jax.shard_map(
        make_local(sizes),
        mesh=mesh,
        in_specs=(P(("groups", "pix", "sub", "inner"), None),),
        out_specs=P(("pix", "sub"), "groups", "inner"),
        check_vma=False,
    )
```

profile of v0, /device:TPU:0, one launch (start us, length us, event | category | flops | bytes accessed | tf_op | source)
XLA Modules:
  0.0 79.0 jit_solution(11939756387512066337)
XLA Ops:
  0.0 1.4 %fusion.49 = f32[256,256]{1,0:T(8,128)S(1)} fusion(bf16[640,256]{1,0:T(8,128)(2,1)} %param.4), kind=kOutput, calls=%fused_computation.78 | convolution fusion | flops 83886080 | bytes 589824 | tf_op jit(solution)/shard_map/dot_general | solution.py:88
  1.4 0.6 collective-permute-start
  2.0 1.1 %collective-permute-done = f32[384,128]{1,0:T(8,128)S(1)} collective-permute-done((f32[384,128]{1,0:T(8,128)S(1)}, f32[384,128]{1,0:T(8,128)S(1)}, u32[]{:S(2)}, u32[]{:S(2)}) %collective-permute-start) | collective-permute-done | bytes 196640 | tf_op jit(solution)/shard_map/ppermute | solution.py:48
  3.1 2.9 %collective-permute-start.1 = (f32[384,128]{1,0:T(8,128)S(1)}, f32[384,128]{1,0:T(8,128)S(1)}, u32[]{:S(2)}, u32[]{:S(2)}) collective-permute-start(f32[384,128]{1,0:T(8,128)S(1)} %fusion.44), channel_id=1, source_target_pairs={{0,2},{2,0},{1,3},{3,1},{4,6},{6,4},{5,7},{7,5},{8,10},{10,8},{9,1... | collective-permute-start | bytes 589832 | tf_op jit(solution)/shard_map/ppermute | solution.py:48
  6.0 5.2 %collective-permute-done.1 = f32[384,128]{1,0:T(8,128)S(1)} collective-permute-done((f32[384,128]{1,0:T(8,128)S(1)}, f32[384,128]{1,0:T(8,128)S(1)}, u32[]{:S(2)}, u32[]{:S(2)}) %collective-permute-start.1) | collective-permute-done | bytes 196640 | tf_op jit(solution)/shard_map/ppermute | solution.py:48
  11.2 1.9 %collective-permute-start.2 = (f32[384,128]{1,0:T(8,128)S(1)}, f32[384,128]{1,0:T(8,128)S(1)}, u32[]{:S(2)}, u32[]{:S(2)}) collective-permute-start(f32[384,128]{1,0:T(8,128)S(1)} %add.30), channel_id=1, source_target_pairs={{0,4},{4,0},{8,12},{12,8},{1,5},{5,1},{9,13},{13,9},{2,6},{6,2},{1... | collective-permute-start | bytes 589832 | tf_op jit(solution)/shard_map/ppermute | solution.py:48
  13.1 4.5 %collective-permute-done.2 = f32[384,128]{1,0:T(8,128)S(1)} collective-permute-done((f32[384,128]{1,0:T(8,128)S(1)}, f32[384,128]{1,0:T(8,128)S(1)}, u32[]{:S(2)}, u32[]{:S(2)}) %collective-permute-start.2) | collective-permute-done | bytes 196640 | tf_op jit(solution)/shard_map/ppermute | solution.py:48
  17.7 2.6 %collective-permute-start.3 = (f32[384,128]{1,0:T(8,128)S(1)}, f32[384,128]{1,0:T(8,128)S(1)}, u32[]{:S(2)}, u32[]{:S(2)}) collective-permute-start(f32[384,128]{1,0:T(8,128)S(1)} %add.31), channel_id=1, source_target_pairs={{0,8},{4,12},{8,0},{12,4},{1,9},{5,13},{9,1},{13,5},{2,10},{6,14},... | collective-permute-start | bytes 589832 | tf_op jit(solution)/shard_map/ppermute | solution.py:48
  20.3 8.1 %collective-permute-done.3 = f32[384,128]{1,0:T(8,128)S(1)} collective-permute-done((f32[384,128]{1,0:T(8,128)S(1)}, f32[384,128]{1,0:T(8,128)S(1)}, u32[]{:S(2)}, u32[]{:S(2)}) %collective-permute-start.3) | collective-permute-done | bytes 196640 | tf_op jit(solution)/shard_map/ppermute | solution.py:48
  28.4 0.1 copy.15
  28.5 0.3 fusion.13
  28.8 0.2 fusion.50
  29.0 0.1 copy.16
  29.1 2.9 %cholesky.74 = f32[32,32]{1,0:T(8,128)S(1)} custom-call(f32[32,32]{1,0:T(8,128)S(1)} %fusion.32), custom_call_target="Cholesky" | custom-call | tf_op jit(solution)/shard_map/jit(cholesky)/cholesky | solution.py:21
  32.0 0.6 compare_reduce_fusion.3
  32.7 0.7 fusion.21
  33.3 2.4 %custom-call.8 = f32[1,32,32]{1,2,0:T(8,128)S(1)} custom-call(f32[1,32,32]{2,1,0:T(8,128)S(1)} %fusion.21), custom_call_target="InvertDiagBlocksLowerTriangular" | custom-call | tf_op jit(solution)/shard_map/jit(_solve_triangular)/triangular_solve | solution.py:22
  35.7 0.2 fusion.19
  36.0 0.3 fusion.47
  36.4 0.2 fusion.51
  36.5 0.1 copy.17
  36.6 2.9 %cholesky.85 = f32[32,32]{1,0:T(8,128)S(1)} custom-call(f32[32,32]{1,0:T(8,128)S(1)} %fusion.30), custom_call_target="Cholesky" | custom-call | tf_op jit(solution)/shard_map/jit(cholesky)/cholesky | solution.py:21
  39.6 0.6 compare_reduce_fusion.2
  40.2 0.7 fusion.22
  40.9 2.4 %custom-call.9 = f32[1,32,32]{1,2,0:T(8,128)S(1)} custom-call(f32[1,32,32]{2,1,0:T(8,128)S(1)} %fusion.22), custom_call_target="InvertDiagBlocksLowerTriangular" | custom-call | tf_op jit(solution)/shard_map/jit(_solve_triangular)/triangular_solve | solution.py:22
  43.3 0.2 fusion.17
  43.5 0.3 fusion.46
  43.9 0.2 fusion.52
  44.1 0.1 copy.18
  44.1 2.9 %cholesky.96 = f32[32,32]{1,0:T(8,128)S(1)} custom-call(f32[32,32]{1,0:T(8,128)S(1)} %fusion.28), custom_call_target="Cholesky" | custom-call | tf_op jit(solution)/shard_map/jit(cholesky)/cholesky | solution.py:21
  47.1 0.6 compare_reduce_fusion.1
  47.7 0.7 fusion.23
  48.4 2.4 %custom-call.10 = f32[1,32,32]{1,2,0:T(8,128)S(1)} custom-call(f32[1,32,32]{2,1,0:T(8,128)S(1)} %fusion.23), custom_call_target="InvertDiagBlocksLowerTriangular" | custom-call | tf_op jit(solution)/shard_map/jit(_solve_triangular)/triangular_solve | solution.py:22
  50.8 0.2 fusion.15
  51.1 0.0 copy-start
  51.1 0.3 fusion.45
  51.5 0.2 fusion.53
  51.6 0.1 copy.19
  51.7 2.9 %cholesky.107 = f32[32,32]{1,0:T(8,128)S(1)} custom-call(f32[32,32]{1,0:T(8,128)S(1)} %fusion.26), custom_call_target="Cholesky" | custom-call | tf_op jit(solution)/shard_map/jit(cholesky)/cholesky | solution.py:21
  54.7 0.6 compare_reduce_fusion
  55.3 0.7 fusion.24
  56.0 2.4 %custom-call.11 = f32[1,32,32]{1,2,0:T(8,128)S(1)} custom-call(f32[1,32,32]{2,1,0:T(8,128)S(1)} %fusion.24), custom_call_target="InvertDiagBlocksLowerTriangular" | custom-call | tf_op jit(solution)/shard_map/jit(_solve_triangular)/triangular_solve | solution.py:22
  58.4 0.2 convolution_convert_fusion.2
  58.6 0.0 copy-done
  58.7 0.2 convolution_convert_fusion.1
  58.9 1.5 %fusion.1 = bf16[256,1,640]{2,0,1:T(8,128)(2,1)S(1)} fusion(bf16[32,640]{1,0:T(8,128)(2,1)S(1)} %convolution_convert_fusion.1, bf16[32,256]{1,0:T(8,128)(2,1)S(1)} %convolution_convert_fusion.2, bf16[640,256]{1,0:T(8,128)(2,1)S(1)} %copy-done, s32[256]{0:T(256)S(1)} %iota_add_fusion, pred[256]{0:T(512)(128)(4,1)S(1)} %iota_compare_fusion.4), kind=kOutput, calls=%fused_computation.3 | convolution fusion | flops 96206848 | bytes 713984 | tf_op jit(solution)/shard_map/dot_general | solution.py:100
  60.4 0.5 broadcast.63
  60.9 0.8 %reduce.4 = bf16[256,640]{1,0:T(8,128)(2,1)S(1)} reduce(bf16[256,1,640]{2,0,1:T(8,128)(2,1)S(1)} %fusion.1, bf16[]{:T(256)} %broadcast.63), dimensions={1}, to_apply=%copy.20.reduce_sub_computation | reduce | bytes 655362 | tf_op jit(solution)/shard_map/broadcast_in_dim | solution.py:104
  61.7 0.1 reshape.8
  61.8 16.0 %all_to_all.18 = bf16[8,2,10240]{2,1,0:T(2,128)(2,1)S(1)} all-to-all(bf16[8,2,10240]{2,1,0:T(2,128)(2,1)S(1)} %reshape.8), channel_id=1, replica_groups=mesh['groups'=2,'pix'=4,'sub'=2,'inner'=2] {'pix','sub'}, dimensions={0} | all-to-all | bytes 655360 | tf_op jit(solution)/shard_map/all_to_all | solution.py:103
  77.8 0.3 reshape.9
  78.2 0.8 %copy.21 = bf16[32,8,640]{2,1,0:T(8,128)(2,1)} copy(bf16[32,8,640]{2,0,1:T(8,128)(2,1)S(1)} %bitcast.74) | data formatting | bytes 655360 | tf_op jit(solution)/shard_map/all_to_all | solution.py:103
  (19 shorter events, 0.3 us)
Async XLA Ops:
  1.4 1.6 %collective-permute-start = (f32[384,128]{1,0:T(8,128)S(1)}, f32[384,128]{1,0:T(8,128)S(1)}, u32[]{:S(2)}, u32[]{:S(2)}) collective-permute-start(f32[384,128]{1,0:T(8,128)S(1)} %pad_maximum_fusion), channel_id=1, source_target_pairs={{0,1},{1,0},{2,3},{3,2},{4,5},{5,4},{6,7},{7,6},{8,9},{9,8},{10,11... | collective-permute-start | bytes 589832 | tf_op jit(solution)/shard_map/ppermute | solution.py:48
  3.1 8.1 %collective-permute-start.1 = (f32[384,128]{1,0:T(8,128)S(1)}, f32[384,128]{1,0:T(8,128)S(1)}, u32[]{:S(2)}, u32[]{:S(2)}) collective-permute-start(f32[384,128]{1,0:T(8,128)S(1)} %fusion.44), channel_id=1, source_target_pairs={{0,2},{2,0},{1,3},{3,1},{4,6},{6,4},{5,7},{7,5},{8,10},{10,8},{9,1... | collective-permute-start | bytes 589832 | tf_op jit(solution)/shard_map/ppermute | solution.py:48
  11.2 6.4 %collective-permute-start.2 = (f32[384,128]{1,0:T(8,128)S(1)}, f32[384,128]{1,0:T(8,128)S(1)}, u32[]{:S(2)}, u32[]{:S(2)}) collective-permute-start(f32[384,128]{1,0:T(8,128)S(1)} %add.30), channel_id=1, source_target_pairs={{0,4},{4,0},{8,12},{12,8},{1,5},{5,1},{9,13},{13,9},{2,6},{6,2},{1... | collective-permute-start | bytes 589832 | tf_op jit(solution)/shard_map/ppermute | solution.py:48
  17.7 10.7 %collective-permute-start.3 = (f32[384,128]{1,0:T(8,128)S(1)}, f32[384,128]{1,0:T(8,128)S(1)}, u32[]{:S(2)}, u32[]{:S(2)}) collective-permute-start(f32[384,128]{1,0:T(8,128)S(1)} %add.31), channel_id=1, source_target_pairs={{0,8},{4,12},{8,0},{12,4},{1,9},{5,13},{9,1},{13,5},{2,10},{6,14},... | collective-permute-start | bytes 589832 | tf_op jit(solution)/shard_map/ppermute | solution.py:48
  51.1 7.6 %copy-start = (bf16[640,256]{1,0:T(8,128)(2,1)S(1)}, bf16[640,256]{1,0:T(8,128)(2,1)}, u32[]{:S(2)}) copy-start(bf16[640,256]{1,0:T(8,128)(2,1)} %param.4) | copy-start | bytes 983044
where the time goes:
time: 79.2 us; the launch traced here: 79 us
  other arithmetic  27.7 us (35%)
  waiting for transfers between devices  18.9 us (24%)
  blocking collectives  16 us (20%)
  starting transfers between devices  7.98 us (10%)
  matrix products  6.01 us (8%)
  local copies, waits for them, and re-layouts  2.2 us (3%)
    ppermute x4, waiting for transfers between devices, butterfly_sum(): x = x + lax.ppermute(x, name, [(i, i ^ d) for i in range(n)])  18.9 us
    all_to_all x1, blocking collectives, local(): lax.all_to_all(coefficients[:, None, :], ('pix', 'sub'), split_axis=0, co...  16 us
    another operation x12, other arithmetic, leading_modes(): lower_factor = jnp.linalg.cholesky(cross_gram)  14.4 us
    another operation x8, other arithmetic, leading_modes(): jax.scipy.linalg.solve_triangular(lower_factor, product.T, lower=True)  12.3 us
    ppermute x4, starting transfers between devices, butterfly_sum(): x = x + lax.ppermute(x, name, [(i, i ^ d) for i in range(n)])  7.98 us
    dot_general x8, matrix products, matmul_high(): return jnp.dot(left, right, precision=lax.Precision.HIGHEST)  1.94 us
  transfers between devices with their start and end apart: 4, of which 4 were waited for; matrix products, arithmetic and copies ran while one was open for 0% of the time, Pallas kernels for 0%

commit v1 on v0

--- a/solution.py
+++ b/solution.py
@@ -100,8 +100,16 @@
         coefficients = lax.dot_general(
             table_b, cleaned, (((1,), (1,)), ((), ())), preferred_element_type=jnp.float32
         ).astype(jnp.bfloat16)
-        spectra = lax.all_to_all(
-            coefficients[:, None, :], ("pix", "sub"), split_axis=0, concat_axis=1, tiled=True
+        spectra = jnp.concatenate(
+            lax.all_to_all(
+                jnp.stack(
+                    jnp.split(coefficients[:, None, :], lax.axis_size(("pix", "sub")), axis=0)
+                ),
+                ("pix", "sub"),
+                0,
+                0,
+            ),
+            axis=1,
         )
         return spectra
 

time: 79.2 us -> 77.5 us (0.979)
  local copies, waits for them, and re-layouts: 2.2 us -> 1.33 us
  other arithmetic: 27.7 us -> 26.9 us
    all_to_all x1 -> x0, local copies, waits for them, and re-layouts: 0.83 us -> none  [local(): lax.all_to_all(coefficients[:, None, :], ('pix', 'sub'), split_axis=0, co...]
    reshape x0 -> x1, local copies, waits for them, and re-layouts: none -> 0.83 us  [local(): jnp.concatenate(lax.all_to_all(jnp.stack(jnp.split(coefficients[:, None,...]
    broadcast_in_dim x1 -> x0, other arithmetic: 0.82 us -> none  [local(): coefficients[:, None, :]]
where the time goes in v1:
time: 77.5 us; the launch traced here: 77.3 us
  other arithmetic  26.9 us (35%)
  waiting for transfers between devices  18.9 us (24%)
  blocking collectives  16 us (21%)
  starting transfers between devices  7.98 us (10%)
  matrix products  6.01 us (8%)
  local copies, waits for them, and re-layouts  1.33 us (2%)
    ppermute x4, waiting for transfers between devices, butterfly_sum(): x = x + lax.ppermute(x, name, [(i, i ^ d) for i in range(n)])  18.9 us
    all_to_all x1, blocking collectives, local(): lax.all_to_all(jnp.stack(jnp.split(coefficients[:, None, :], lax.axis_siz...  16 us
    another operation x12, other arithmetic, leading_modes(): lower_factor = jnp.linalg.cholesky(cross_gram)  14.4 us
    another operation x8, other arithmetic, leading_modes(): jax.scipy.linalg.solve_triangular(lower_factor, product.T, lower=True)  12.3 us
    ppermute x4, starting transfers between devices, butterfly_sum(): x = x + lax.ppermute(x, name, [(i, i ^ d) for i in range(n)])  7.98 us
    dot_general x8, matrix products, matmul_high(): return jnp.dot(left, right, precision=lax.Precision.HIGHEST)  1.94 us
  transfers between devices with their start and end apart: 4, of which 4 were waited for; matrix products, arithmetic and copies ran while one was open for 0% of the time, Pallas kernels for 0%

profile of v1, /device:TPU:0, one launch (start us, length us, event | category | flops | bytes accessed | tf_op | source)
XLA Modules:
  0.0 77.3 jit_solution(16545306248271003670)
XLA Ops:
  0.0 1.4 %fusion.56 = f32[256,256]{1,0:T(8,128)S(1)} fusion(bf16[640,256]{1,0:T(8,128)(2,1)} %param.4), kind=kOutput, calls=%fused_computation.93 | convolution fusion | flops 83886080 | bytes 589824 | tf_op jit(solution)/shard_map/dot_general | solution.py:88
  1.4 0.6 collective-permute-start
  2.0 1.1 %collective-permute-done = f32[384,128]{1,0:T(8,128)S(1)} collective-permute-done((f32[384,128]{1,0:T(8,128)S(1)}, f32[384,128]{1,0:T(8,128)S(1)}, u32[]{:S(2)}, u32[]{:S(2)}) %collective-permute-start) | collective-permute-done | bytes 196640 | tf_op jit(solution)/shard_map/ppermute | solution.py:48
  3.1 2.9 %collective-permute-start.1 = (f32[384,128]{1,0:T(8,128)S(1)}, f32[384,128]{1,0:T(8,128)S(1)}, u32[]{:S(2)}, u32[]{:S(2)}) collective-permute-start(f32[384,128]{1,0:T(8,128)S(1)} %fusion.51), channel_id=1, source_target_pairs={{0,2},{2,0},{1,3},{3,1},{4,6},{6,4},{5,7},{7,5},{8,10},{10,8},{9,1... | collective-permute-start | bytes 589832 | tf_op jit(solution)/shard_map/ppermute | solution.py:48
  6.0 5.2 %collective-permute-done.1 = f32[384,128]{1,0:T(8,128)S(1)} collective-permute-done((f32[384,128]{1,0:T(8,128)S(1)}, f32[384,128]{1,0:T(8,128)S(1)}, u32[]{:S(2)}, u32[]{:S(2)}) %collective-permute-start.1) | collective-permute-done | bytes 196640 | tf_op jit(solution)/shard_map/ppermute | solution.py:48
  11.2 1.9 %collective-permute-start.2 = (f32[384,128]{1,0:T(8,128)S(1)}, f32[384,128]{1,0:T(8,128)S(1)}, u32[]{:S(2)}, u32[]{:S(2)}) collective-permute-start(f32[384,128]{1,0:T(8,128)S(1)} %add.30), channel_id=1, source_target_pairs={{0,4},{4,0},{8,12},{12,8},{1,5},{5,1},{9,13},{13,9},{2,6},{6,2},{1... | collective-permute-start | bytes 589832 | tf_op jit(solution)/shard_map/ppermute | solution.py:48
  13.1 4.5 %collective-permute-done.2 = f32[384,128]{1,0:T(8,128)S(1)} collective-permute-done((f32[384,128]{1,0:T(8,128)S(1)}, f32[384,128]{1,0:T(8,128)S(1)}, u32[]{:S(2)}, u32[]{:S(2)}) %collective-permute-start.2) | collective-permute-done | bytes 196640 | tf_op jit(solution)/shard_map/ppermute | solution.py:48
  17.7 2.6 %collective-permute-start.3 = (f32[384,128]{1,0:T(8,128)S(1)}, f32[384,128]{1,0:T(8,128)S(1)}, u32[]{:S(2)}, u32[]{:S(2)}) collective-permute-start(f32[384,128]{1,0:T(8,128)S(1)} %add.31), channel_id=1, source_target_pairs={{0,8},{4,12},{8,0},{12,4},{1,9},{5,13},{9,1},{13,5},{2,10},{6,14},... | collective-permute-start | bytes 589832 | tf_op jit(solution)/shard_map/ppermute | solution.py:48
  20.3 8.1 %collective-permute-done.3 = f32[384,128]{1,0:T(8,128)S(1)} collective-permute-done((f32[384,128]{1,0:T(8,128)S(1)}, f32[384,128]{1,0:T(8,128)S(1)}, u32[]{:S(2)}, u32[]{:S(2)}) %collective-permute-start.3) | collective-permute-done | bytes 196640 | tf_op jit(solution)/shard_map/ppermute | solution.py:48
  28.4 0.1 copy.2
  28.5 0.3 fusion.12
  28.8 0.2 fusion.57
  29.0 0.1 copy.3
  29.1 2.9 %cholesky.74 = f32[32,32]{1,0:T(8,128)S(1)} custom-call(f32[32,32]{1,0:T(8,128)S(1)} %fusion.39), custom_call_target="Cholesky" | custom-call | tf_op jit(solution)/shard_map/jit(cholesky)/cholesky | solution.py:21
  32.0 0.6 compare_reduce_fusion.3
  32.7 0.7 fusion.28
  33.3 2.4 %custom-call.8 = f32[1,32,32]{1,2,0:T(8,128)S(1)} custom-call(f32[1,32,32]{2,1,0:T(8,128)S(1)} %fusion.28), custom_call_target="InvertDiagBlocksLowerTriangular" | custom-call | tf_op jit(solution)/shard_map/jit(_solve_triangular)/triangular_solve | solution.py:22
  35.7 0.2 fusion.26
  36.0 0.3 fusion.54
  36.4 0.2 fusion.58
  36.5 0.1 copy.4
  36.6 2.9 %cholesky.85 = f32[32,32]{1,0:T(8,128)S(1)} custom-call(f32[32,32]{1,0:T(8,128)S(1)} %fusion.37), custom_call_target="Cholesky" | custom-call | tf_op jit(solution)/shard_map/jit(cholesky)/cholesky | solution.py:21
  39.6 0.6 compare_reduce_fusion.2
  40.2 0.7 fusion.29
  40.9 2.4 %custom-call.9 = f32[1,32,32]{1,2,0:T(8,128)S(1)} custom-call(f32[1,32,32]{2,1,0:T(8,128)S(1)} %fusion.29), custom_call_target="InvertDiagBlocksLowerTriangular" | custom-call | tf_op jit(solution)/shard_map/jit(_solve_triangular)/triangular_solve | solution.py:22
  43.3 0.2 fusion.24
  43.5 0.3 fusion.53
  43.9 0.2 fusion.59
  44.1 0.1 copy.5
  44.1 2.9 %cholesky.96 = f32[32,32]{1,0:T(8,128)S(1)} custom-call(f32[32,32]{1,0:T(8,128)S(1)} %fusion.35), custom_call_target="Cholesky" | custom-call | tf_op jit(solution)/shard_map/jit(cholesky)/cholesky | solution.py:21
  47.1 0.6 compare_reduce_fusion.1
  47.7 0.7 fusion.30
  48.4 2.4 %custom-call.10 = f32[1,32,32]{1,2,0:T(8,128)S(1)} custom-call(f32[1,32,32]{2,1,0:T(8,128)S(1)} %fusion.30), custom_call_target="InvertDiagBlocksLowerTriangular" | custom-call | tf_op jit(solution)/shard_map/jit(_solve_triangular)/triangular_solve | solution.py:22
  50.8 0.2 fusion.22
  51.1 0.0 copy-start
  51.1 0.3 fusion.52
  51.5 0.2 fusion.60
  51.6 0.1 copy.6
  51.7 2.9 %cholesky.107 = f32[32,32]{1,0:T(8,128)S(1)} custom-call(f32[32,32]{1,0:T(8,128)S(1)} %fusion.33), custom_call_target="Cholesky" | custom-call | tf_op jit(solution)/shard_map/jit(cholesky)/cholesky | solution.py:21
  54.7 0.6 compare_reduce_fusion
  55.3 0.7 fusion.31
  56.0 2.4 %custom-call.11 = f32[1,32,32]{1,2,0:T(8,128)S(1)} custom-call(f32[1,32,32]{2,1,0:T(8,128)S(1)} %fusion.31), custom_call_target="InvertDiagBlocksLowerTriangular" | custom-call | tf_op jit(solution)/shard_map/jit(_solve_triangular)/triangular_solve | solution.py:22
  58.4 0.2 convolution_convert_fusion.2
  58.6 0.0 copy-done
  58.7 0.2 convolution_convert_fusion.1
  58.9 1.5 %convolution_convert_fusion = bf16[256,640]{1,0:T(8,128)(2,1)S(1)} fusion(bf16[32,640]{1,0:T(8,128)(2,1)S(1)} %convolution_convert_fusion.1, bf16[32,256]{1,0:T(8,128)(2,1)S(1)} %convolution_convert_fusion.2, bf16[640,256]{1,0:T(8,128)(2,1)S(1)} %copy-done, s32[256]{0:T(256)S(1)} %iota_add_fusion, pred[256]{0:T(512)(128)(4,1)S(1)} %iota_compare_fusion.4), kind=kOutput, calls=%fused_computation.1 | convolution fusion | flops 96206848 | bytes 713984 | tf_op jit(solution)/shard_map/dot_general | solution.py:100
  60.5 16.0 %all_to_all.5 = bf16[8,32,1,640]{3,1,2,0:T(8,128)(2,1)S(1)} all-to-all(bf16[8,32,1,640]{3,1,2,0:T(8,128)(2,1)S(1)} %fusion.13), channel_id=1, replica_groups=mesh['groups'=2,'pix'=4,'sub'=2,'inner'=2] {'pix','sub'}, dimensions={0} | all-to-all | bytes 655360 | tf_op jit(solution)/shard_map/all_to_all | solution.py:104
  76.5 0.8 %copy.7 = bf16[32,8,640]{2,1,0:T(8,128)(2,1)} copy(bf16[32,8,640]{2,0,1:T(8,128)(2,1)S(1)} %bitcast.102) | data formatting | bytes 655360 | tf_op jit(solution)/shard_map/reshape | solution.py:103
  (26 shorter events, 0.4 us)
Async XLA Ops:
  1.4 1.6 %collective-permute-start = (f32[384,128]{1,0:T(8,128)S(1)}, f32[384,128]{1,0:T(8,128)S(1)}, u32[]{:S(2)}, u32[]{:S(2)}) collective-permute-start(f32[384,128]{1,0:T(8,128)S(1)} %pad_maximum_fusion), channel_id=1, source_target_pairs={{0,1},{1,0},{2,3},{3,2},{4,5},{5,4},{6,7},{7,6},{8,9},{9,8},{10,11... | collective-permute-start | bytes 589832 | tf_op jit(solution)/shard_map/ppermute | solution.py:48
  3.1 8.1 %collective-permute-start.1 = (f32[384,128]{1,0:T(8,128)S(1)}, f32[384,128]{1,0:T(8,128)S(1)}, u32[]{:S(2)}, u32[]{:S(2)}) collective-permute-start(f32[384,128]{1,0:T(8,128)S(1)} %fusion.51), channel_id=1, source_target_pairs={{0,2},{2,0},{1,3},{3,1},{4,6},{6,4},{5,7},{7,5},{8,10},{10,8},{9,1... | collective-permute-start | bytes 589832 | tf_op jit(solution)/shard_map/ppermute | solution.py:48
  11.2 6.4 %collective-permute-start.2 = (f32[384,128]{1,0:T(8,128)S(1)}, f32[384,128]{1,0:T(8,128)S(1)}, u32[]{:S(2)}, u32[]{:S(2)}) collective-permute-start(f32[384,128]{1,0:T(8,128)S(1)} %add.30), channel_id=1, source_target_pairs={{0,4},{4,0},{8,12},{12,8},{1,5},{5,1},{9,13},{13,9},{2,6},{6,2},{1... | collective-permute-start | bytes 589832 | tf_op jit(solution)/shard_map/ppermute | solution.py:48
  17.7 10.7 %collective-permute-start.3 = (f32[384,128]{1,0:T(8,128)S(1)}, f32[384,128]{1,0:T(8,128)S(1)}, u32[]{:S(2)}, u32[]{:S(2)}) collective-permute-start(f32[384,128]{1,0:T(8,128)S(1)} %add.31), channel_id=1, source_target_pairs={{0,8},{4,12},{8,0},{12,4},{1,9},{5,13},{9,1},{13,5},{2,10},{6,14},... | collective-permute-start | bytes 589832 | tf_op jit(solution)/shard_map/ppermute | solution.py:48
  51.1 7.6 %copy-start = (bf16[640,256]{1,0:T(8,128)(2,1)S(1)}, bf16[640,256]{1,0:T(8,128)(2,1)}, u32[]{:S(2)}) copy-start(bf16[640,256]{1,0:T(8,128)(2,1)} %param.4) | copy-start | bytes 983044
